TPU v7x, 128 devices: a whole 4x4x4 slice. The times are simulated.
128 devices in a mesh: grp: 8 (over x, core), mem: 16 (over z, y).
Axes of the slice: x: 4, y: 4, z: 4, core: 2. Of those that a mesh axis runs over, the one named last changes fastest.
Arguments:
- clips: bfloat16 [32768, 1152], P(('grp', 'mem')), may hold values from -6 to 6
- captions: bfloat16 [8192, 1152], P(('grp', 'mem')), may hold values from -6 to 6
- clip_bucket: int32 [32768], P(('grp', 'mem')), may hold values from 0 to 15, as said below
- clip_positive: int32 [32768], P(('grp', 'mem')), may hold values from 0 to 8191, as said below
- caption_bucket: int32 [8192], P(('grp', 'mem')), may hold values from 0 to 15, as said below
- bucket_owner: int32 [16], replicated, may hold values from 0 to 7, as said below
- scale: float32 [1], replicated, may hold values from 0.02 to 0.06
- bias: float32 [1], replicated, may hold values from -4 to -1
Outputs:
- clip_grad: float32 [32768, 1152], P(('grp', 'mem'))
- caption_grad: float32 [8192, 1152], P(('grp', 'mem'))
Inputs may be any that keep to these rules, and one draw needn't show every extreme that they name: `bucket_owner`: each group owns exactly 2 buckets. `caption_bucket`: caption rows g * 1024 to (g + 1) * 1024 - 1 have buckets owned by group g, and every bucket has a caption. `clip_bucket`: within one device's block of 256 clip rows, among the rows whose offsets in the block are equal modulo the size of axis mem, at most 4 have buckets owned by one group; one group receives exactly 4 such rows from every such set of every device. `clip_positive`: each clip's own caption has the clip's bucket.
All inputs are finite; a program needn't handle non-finite values.
Results may differ from a plain program's by a relative error of at most 0.0027.
Values may be sent and summed in bfloat16 or wider, within the bound.
No kernel may reach another device: no remote copies, remote signals or barrier semaphores. Data moves between devices by JAX's collectives and lax.ppermute only.
A program may use at most 128 MiB of HBM per device.

v0:
```python
import jax
import jax.numpy as jnp
from jax import lax
from jax.sharding import PartitionSpec as P


def pair_weights(logits, matched, same):
    sign = jnp.where(matched, 1.0, -1.0).astype(jnp.float32)
    return jnp.where(same, -sign * jax.nn.sigmoid(-sign * logits), 0.0).astype(jnp.bfloat16)


def inner_rows(left, right):
    return lax.dot_general(
        left, right, (((1,), (1,)), ((), ())), preferred_element_type=jnp.float32
    )


def body(clips, captions, clip_bucket, clip_positive, caption_bucket, bucket_owner, scale, bias):
    groups = lax.axis_size("grp")
    members = lax.axis_size("mem")
    devices = groups * members
    clip_rows, width = clips.shape
    cap_rows = captions.shape[0]
    capacity = 2 * clip_rows // devices
    slots = capacity * devices
    panel = cap_rows * members
    mult = scale[0]
    shift = bias[0]
    local = jnp.arange(clip_rows, dtype=jnp.int32)
    target = bucket_owner[clip_bucket] * members + local % members
    onehot = (target[:, None] == jnp.arange(devices, dtype=jnp.int32)[None, :]).astype(jnp.float32)
    earlier = (local[None, :] < local[:, None]).astype(jnp.float32)
    before = jnp.dot(earlier, onehot, preferred_element_type=jnp.float32)
    rank = jnp.sum(before * onehot, axis=1).astype(jnp.int32)
    position = target * capacity + rank
    send_rows = jnp.zeros((slots, width), clips.dtype).at[position].set(clips)
    send_bucket = jnp.full((slots,), -1, jnp.int32).at[position].set(clip_bucket)
    send_positive = jnp.full((slots,), -1, jnp.int32).at[position].set(clip_positive)
    recv_rows, recv_bucket, recv_positive = (
        lax.all_to_all(send_rows, ("grp", "mem"), split_axis=0, concat_axis=0, tiled=True),
        lax.all_to_all(send_bucket, ("grp", "mem"), split_axis=0, concat_axis=0, tiled=True),
        lax.all_to_all(send_positive, ("grp", "mem"), split_axis=0, concat_axis=0, tiled=True),
    )
    group_index = lax.axis_index("grp")
    rows_y = lax.all_gather(captions, "mem", axis=0, tiled=True)
    bucket_y = lax.all_gather(caption_bucket, "mem", axis=0, tiled=True)
    count = rows_y.shape[0]
    logits = mult * inner_rows(recv_rows, rows_y) + shift
    ids = group_index * panel + jnp.arange(count, dtype=jnp.int32)
    weight = pair_weights(
        logits, recv_positive[:, None] == ids[None, :], recv_bucket[:, None] == bucket_y[None, :]
    )
    total = jnp.dot(weight, rows_y, preferred_element_type=jnp.float32)
    caption_grad = lax.psum_scatter(
        lax.dot_general(
            weight, recv_rows, (((0,), (0,)), ((), ())), preferred_element_type=jnp.float32
        ),
        "mem",
        scatter_dimension=0,
        tiled=True,
    )
    returned = lax.all_to_all(total, ("grp", "mem"), split_axis=0, concat_axis=0, tiled=True)
    clip_grad = returned[position]
    return (clip_grad, caption_grad)


def solution(mesh):
    placed = (
        P(("grp", "mem"), None),
        P(("grp", "mem"), None),
        P(("grp", "mem")),
        P(("grp", "mem")),
        P(("grp", "mem")),
        P(),
        P(),
        P(),
    )
    return jax.shard_map(
        body,
        mesh=mesh,
        in_specs=placed,
        out_specs=(P(("grp", "mem"), None), P(("grp", "mem"), None)),
        check_vma=False,
    )
```

profile of v0, /device:TPU:0, one launch (start us, length us, event | category | flops | bytes accessed | tf_op | source)
XLA Modules:
  0.0 204.4 jit_solution(15715490351889478271)
XLA Ops:
  7.2 0.0 all-gather.2.cloned.1.call-start
  7.2 0.7 all-gather.2.cloned.1.call-update
  7.9 1.9 fusion.12
  9.9 10.7 %fusion.5 = (s32[256]{0:T(256)S(1)}, s32[256]{0:T(256)S(1)}) fusion(s32[]{:T(128)} %bitcast.15, s32[]{:T(128)} %bitcast.14, s32[]{:T(128)} %bitcast.13, s32[]{:T(128)} %bitcast.12, s32[]{:T(128)} %bitcast.11, s32[]{:T(128)} %bitcast.10, s32[]{:T(128)} %bitcast.9, s32[]{:T(128)} %bitcast.8, s32[]{:T(128)} %bitcast.7, s32[]{:T(128)} %bitcast.6, s32[]{:T(128)} %bitcast.5, ...), kind=kLoop, calls=%fused_computation.34 | loop fusion | flops 10496 | bytes 3136 | tf_op jit(solution)/shard_map/add | solution.py:30
  20.6 0.2 fusion
  20.8 1.6 scatter_custom_fusion
  22.4 0.7 all_to_all.28
  23.1 11.2 %all-to-all-start = ((s32[128,4,1]{1,2,0:T(1,128)}), s32[128,4,1]{1,2,0:T(1,128)S(1)}, u32[]{:S(2)}, u32[]{:S(2)}) async-start(s32[128,4,1]{1,2,0:T(1,128)} %bitcast.19), calls=%async_computation | async-start | bytes 131072 | tf_op jit(solution)/shard_map/all_to_all | solution.py:41
  34.3 1.6 scatter_custom_fusion.1
  35.9 0.7 all_to_all.30
  36.6 7.1 %all-to-all-done = s32[128,4,1]{1,2,0:T(1,128)S(1)} async-done(((s32[128,4,1]{1,2,0:T(1,128)}), s32[128,4,1]{1,2,0:T(1,128)S(1)}, u32[]{:S(2)}, u32[]{:S(2)}) %all-to-all-start) | async-done | bytes 2080 | tf_op jit(solution)/shard_map/all_to_all | solution.py:41
  43.7 4.6 %all-to-all-start.1 = ((s32[128,4,1]{1,2,0:T(1,128)}), s32[128,4,1]{1,2,0:T(1,128)S(1)}, u32[]{:S(2)}, u32[]{:S(2)}) async-start(s32[128,4,1]{1,2,0:T(1,128)} %bitcast.21), calls=%async_computation.1 | async-start | bytes 131072 | tf_op jit(solution)/shard_map/all_to_all | solution.py:42
  48.3 2.6 %scatter_custom_fusion.2 = bf16[512,1152]{1,0:T(8,128)(2,1)S(1)} fusion(s32[256]{0:T(256)S(1)} %bitcast.39, bf16[256,1152]{1,0:T(8,128)(2,1)} %param.8, bf16[]{:T(256)} %constant.41.clone.1), kind=kCustom, calls=%fused_computation.7 | custom fusion | bytes 1180160 | tf_op jit(solution)/shard_map/scatter | solution.py:36
  51.0 0.0 copy-start.1
  51.0 0.0 copy-start
  51.0 1.2 all_to_all.32
  52.2 5.6 %all-to-all-done.1 = s32[128,4,1]{1,2,0:T(1,128)S(1)} async-done(((s32[128,4,1]{1,2,0:T(1,128)}), s32[128,4,1]{1,2,0:T(1,128)S(1)}, u32[]{:S(2)}, u32[]{:S(2)}) %all-to-all-start.1) | async-done | bytes 2080 | tf_op jit(solution)/shard_map/all_to_all | solution.py:42
  57.8 4.6 %all-to-all-start.2 = ((bf16[128,4,1152]{2,1,0:T(4,128)(2,1)}), bf16[128,4,1152]{2,1,0:T(4,128)(2,1)S(1)}, u32[]{:S(2)}, u32[]{:S(2)}) async-start(bf16[128,4,1152]{2,1,0:T(4,128)(2,1)} %all_to_all.32), calls=%async_computation.2 | async-start | bytes 2359296 | tf_op jit(solution)/shard_map/all_to_all | solution.py:40
  62.4 0.0 reduce-scatter.2.cloned.1.call-start
  63.8 0.0 copy-done.1
  63.8 0.6 dynamic-slice
  64.9 0.0 copy-done
  65.0 0.2 dynamic-update-slice
  65.2 19.7 %all-reduce = s32[1024]{0:T(1024)S(1)} all-reduce(s32[1024]{0:T(1024)S(1)} %dynamic-update-slice), channel_id=1, replica_groups=mesh['grp'=8,'mem'=16] {'mem'}, use_global_device_ids=true, to_apply=%add | all-reduce | flops 1024 | bytes 8192
  84.9 0.5 broadcast.198
  85.4 0.7 reduce.7
  86.1 0.1 eq.48
  86.2 0.7 reduce.6
  87.0 0.1 eq.52
  87.1 0.0 all-to-all-done.2
  87.1 0.3 all_to_all.34
  87.4 0.0 all-gather.2.cloned.1.call-done
  87.4 3.9 %select_convert_fusion = bf16[512,1024]{1,0:T(8,128)(2,1)S(1)} fusion(bf16[512,1152]{1,0:T(8,128)(2,1)S(1)} %all_to_all.34, bf16[1024,1152]{1,0:T(8,128)(2,1)} %all-gather.2.cloned.1.call-done, f32[]{:T(128)} %bitcast.33, f32[]{:T(128)} %bitcast.32, s32[1024]{0:T(1024)S(1)} %iota_add_fusion, s32[1024]{0:T(1024)S(1)} %all-reduce, s32[512]{0:T(512)S(1)} %eq.52, ...), kind=kOutput, calls=%fused_computation.4 | convolution fusion | flops 1214775296 | bytes 4599816 | tf_op jit(solution)/shard_map/dot_general | solution.py:13
  91.3 3.7 %fusion.14 = f32[1024,1152]{1,0:T(8,128)} fusion(bf16[512,1024]{1,0:T(8,128)(2,1)S(1)} %select_convert_fusion, bf16[512,1152]{1,0:T(8,128)(2,1)S(1)} %all_to_all.34), kind=kOutput, calls=%fused_computation.42 | convolution fusion | flops 1207959552 | bytes 6946816 | tf_op jit(solution)/shard_map/dot_general | solution.py:55
  95.0 0.0 reduce-scatter.2.cloned.1.call-update
  95.0 3.2 %fusion.13 = f32[512,1152]{1,0:T(8,128)S(1)} fusion(bf16[512,1024]{1,0:T(8,128)(2,1)S(1)} %select_convert_fusion, bf16[1024,1152]{1,0:T(8,128)(2,1)} %all-gather.2.cloned.1.call-done), kind=kOutput, calls=%fused_computation.41 | convolution fusion | flops 1207959552 | bytes 5767168 | tf_op jit(solution)/shard_map/dot_general | solution.py:53
  98.2 1.8 all_to_all.35
  100.1 9.5 %all-to-all-start.3 = ((f32[128,4,1152]{2,1,0:T(4,128)}), f32[128,4,1152]{2,1,0:T(4,128)}, u32[]{:S(2)}, u32[]{:S(2)}) async-start(f32[128,4,1152]{2,1,0:T(4,128)} %all_to_all.35), calls=%async_computation.3 | async-start | bytes 4718592 | tf_op jit(solution)/shard_map/all_to_all | solution.py:62
  109.6 34.2 %all-to-all-done.3 = f32[128,4,1152]{2,1,0:T(4,128)} async-done(((f32[128,4,1152]{2,1,0:T(4,128)}), f32[128,4,1152]{2,1,0:T(4,128)}, u32[]{:S(2)}, u32[]{:S(2)}) %all-to-all-start.3) | async-done | bytes 2359328 | tf_op jit(solution)/shard_map/all_to_all | solution.py:62
  143.7 2.7 %all_to_all.37 = f32[512,1152]{1,0:T(8,128)S(1)} reshape(f32[128,4,1152]{2,1,0:T(4,128)} %all-to-all-done.3) | data formatting | bytes 4718592 | tf_op jit(solution)/shard_map/all_to_all | solution.py:62
  146.4 2.2 %gather_fusion = f32[256,1152]{1,0:T(8,128)} fusion(f32[512,1152]{1,0:T(8,128)S(1)} %all_to_all.37, s32[1024]{0:T(1024)S(1)} %pad_clamp_fusion), kind=kCustom, calls=%fused_computation | custom fusion | bytes 2360320 | tf_op jit(solution)/shard_map/gather | solution.py:63
  148.6 49.0 %reduce-scatter.2.cloned.1.call-done = f32[64,1152]{1,0:T(8,128)} async-done(((f32[1024,1152]{1,0:T(8,128)}), f32[64,1152]{1,0:T(8,128)}) %reduce-scatter.2.cloned.1.call-update) | async-done | bytes 294928 | tf_op jit(solution)/shard_map/reduce_scatter | solution.py:54
  (5 shorter events, 0.0 us)
Async XLA Ops:
  7.2 80.3 %all-gather.2.cloned.1.call-start = ((), (), s32[]{:S(2)}) async-start(), calls=%async_computation.5 | async-start | bytes 2506752 | tf_op jit(solution)/shard_map/all_gather | solution.py:45
  23.1 20.6 %all-to-all-start = ((s32[128,4,1]{1,2,0:T(1,128)}), s32[128,4,1]{1,2,0:T(1,128)S(1)}, u32[]{:S(2)}, u32[]{:S(2)}) async-start(s32[128,4,1]{1,2,0:T(1,128)} %bitcast.19), calls=%async_computation | async-start | bytes 131072 | tf_op jit(solution)/shard_map/all_to_all | solution.py:41
  43.7 14.0 %all-to-all-start.1 = ((s32[128,4,1]{1,2,0:T(1,128)}), s32[128,4,1]{1,2,0:T(1,128)S(1)}, u32[]{:S(2)}, u32[]{:S(2)}) async-start(s32[128,4,1]{1,2,0:T(1,128)} %bitcast.21), calls=%async_computation.1 | async-start | bytes 131072 | tf_op jit(solution)/shard_map/all_to_all | solution.py:42
  51.0 12.8 %copy-start.1 = (u32[128]{0:T(128)S(1)}, u32[128]{0:T(128)}, u32[]{:S(2)}) copy-start(u32[128]{0:T(128)} %constant.62) | copy-start | bytes 1540
  51.0 14.0 %copy-start = (s32[64]{0:T(128)S(1)}, s32[64]{0:T(128)}, u32[]{:S(2)}) copy-start(s32[64]{0:T(128)} %param.12) | copy-start | bytes 772
  57.8 29.3 %all-to-all-start.2 = ((bf16[128,4,1152]{2,1,0:T(4,128)(2,1)}), bf16[128,4,1152]{2,1,0:T(4,128)(2,1)S(1)}, u32[]{:S(2)}, u32[]{:S(2)}) async-start(bf16[128,4,1152]{2,1,0:T(4,128)(2,1)} %all_to_all.32), calls=%async_computation.2 | async-start | bytes 2359296 | tf_op jit(solution)/shard_map/all_to_all | solution.py:40
  62.4 135.1 %reduce-scatter.2.cloned.1.call-start = ((), (), s32[]{:S(2)}) async-start(), calls=%async_computation.6 | async-start | bytes 5013504 | tf_op jit(solution)/shard_map/reduce_scatter | solution.py:54
  100.1 43.7 %all-to-all-start.3 = ((f32[128,4,1152]{2,1,0:T(4,128)}), f32[128,4,1152]{2,1,0:T(4,128)}, u32[]{:S(2)}, u32[]{:S(2)}) async-start(f32[128,4,1152]{2,1,0:T(4,128)} %all_to_all.35), calls=%async_computation.3 | async-start | bytes 4718592 | tf_op jit(solution)/shard_map/all_to_all | solution.py:62
Sparse Core Ops, SparseCore 0:
  10.1 48.6 all-gather.1
  95.2 102.3 reduce-scatter.1
where the time goes:
time: 205 us; the launch traced here: 204 us
  waiting for transfers between devices  96.6 us (47%)
  starting transfers between devices  30 us (15%)
  blocking collectives  19.7 us (10%)
  local copies, waits for them, and re-layouts  18.9 us (9%)
  between operations  16.1 us (8%)
  other arithmetic  12.2 us (6%)
  matrix products  11 us (5%)
    reduce_scatter x1, waiting for transfers between devices, body(): lax.psum_scatter(lax.dot_general(weight, recv_rows, (((0,), (0,)), ((), (...  49 us
    all_to_all x1, waiting for transfers between devices, body(): lax.all_to_all(total, ('grp', 'mem'), split_axis=0, concat_axis=0, tiled=...  34.2 us
    unnamed x1, blocking collectives  19.7 us
    all_to_all x1, starting transfers between devices, body(): lax.all_to_all(send_bucket, ('grp', 'mem'), split_axis=0, concat_axis=0,...  11.2 us
    add x1, other arithmetic, body(): target = bucket_owner[clip_bucket] * members + local % members  10.7 us
    all_to_all x1, starting transfers between devices, body(): lax.all_to_all(total, ('grp', 'mem'), split_axis=0, concat_axis=0, tiled=...  9.51 us
    all_to_all x1, waiting for transfers between devices, body(): lax.all_to_all(send_bucket, ('grp', 'mem'), split_axis=0, concat_axis=0,...  7.14 us
    all_to_all x1, waiting for transfers between devices, body(): lax.all_to_all(send_positive, ('grp', 'mem'), split_axis=0, concat_axis=0...  5.62 us
  transfers between devices with their start and end apart: 6, of which 4 were waited for; matrix products, arithmetic and copies ran while one was open for 13% of the time, Pallas kernels for 0%

commit v1 on v0

v1 whole, which is shorter than its diff:
```python
import jax
import jax.numpy as jnp
from jax import lax
from jax.sharding import PartitionSpec as P


def pair_weights(logits, matched, same):
    sign = jnp.where(matched, 1.0, -1.0).astype(jnp.float32)
    return jnp.where(same, -sign * jax.nn.sigmoid(-sign * logits), 0.0).astype(jnp.bfloat16)


def inner_rows(left, right):
    return lax.dot_general(
        left, right, (((1,), (1,)), ((), ())), preferred_element_type=jnp.float32
    )


def body(clips, captions, clip_bucket, clip_positive, caption_bucket, bucket_owner, scale, bias):
    groups = lax.axis_size("grp")
    members = lax.axis_size("mem")
    clip_rows, width = clips.shape
    cap_rows = captions.shape[0]
    n_buckets = bucket_owner.shape[0]
    capacity = clip_rows // members * 4
    slots = capacity * groups
    panel = cap_rows * members
    code_base = panel * groups
    mult = scale[0]
    shift = bias[0]
    bucket_hot = clip_bucket[:, None] == jnp.arange(n_buckets, dtype=jnp.int32)[None, :]
    owner = jnp.sum(jnp.where(bucket_hot, bucket_owner[None, :], 0), axis=1)
    onehot = (owner[:, None] == jnp.arange(groups, dtype=jnp.int32)[None, :]).astype(jnp.int32)
    before = jnp.cumsum(onehot, axis=0) - onehot
    rank = jnp.sum(before * onehot, axis=1)
    position = owner * capacity + rank
    code = clip_bucket * code_base + clip_positive
    send_rows = jnp.zeros((slots, width), clips.dtype).at[position].set(clips)
    send_code = jnp.full((slots,), -1, jnp.int32).at[position].set(code)
    recv_rows = lax.all_to_all(send_rows, "grp", split_axis=0, concat_axis=0, tiled=True)
    recv_code = lax.all_to_all(send_code, "grp", split_axis=0, concat_axis=0, tiled=True)
    recv_bucket = jnp.where(recv_code >= 0, recv_code // code_base, -1)
    recv_positive = jnp.where(recv_code >= 0, recv_code % code_base, -1)
    group_index = lax.axis_index("grp")
    tag = jnp.broadcast_to(caption_bucket.astype(captions.dtype)[:, None], (cap_rows, 128))
    gathered = lax.all_gather(jnp.concatenate([captions, tag], axis=1), "mem", axis=0, tiled=True)
    rows_y = gathered[:, :width]
    bucket_y = gathered[:, width].astype(jnp.int32)
    count = rows_y.shape[0]
    logits = mult * inner_rows(recv_rows, rows_y) + shift
    ids = group_index * panel + jnp.arange(count, dtype=jnp.int32)
    weight = pair_weights(
        logits, recv_positive[:, None] == ids[None, :], recv_bucket[:, None] == bucket_y[None, :]
    )
    total = jnp.dot(weight, rows_y, preferred_element_type=jnp.float32).astype(jnp.bfloat16)
    caption_grad = lax.psum_scatter(
        lax.dot_general(
            weight, recv_rows, (((0,), (0,)), ((), ())), preferred_element_type=jnp.float32
        ),
        "mem",
        scatter_dimension=0,
        tiled=True,
    )
    returned = lax.all_to_all(total, "grp", split_axis=0, concat_axis=0, tiled=True)
    clip_grad = returned[position].astype(jnp.float32)
    return (clip_grad, caption_grad)


def solution(mesh):
    placed = (
        P(("grp", "mem"), None),
        P(("grp", "mem"), None),
        P(("grp", "mem")),
        P(("grp", "mem")),
        P(("grp", "mem")),
        P(),
        P(),
        P(),
    )
    return jax.shard_map(
        body,
        mesh=mesh,
        in_specs=placed,
        out_specs=(P(("grp", "mem"), None), P(("grp", "mem"), None)),
        check_vma=False,
    )
```

time: 205 us -> 154 us (0.75)
  blocking collectives: 19.7 us -> 0 us
  starting transfers between devices: 30 us -> 12.3 us
  local copies, waits for them, and re-layouts: 18.9 us -> 7.59 us
  other arithmetic: 12.2 us -> 7.38 us
  waiting for transfers between devices: 96.6 us -> 99.3 us
    all_gather x1, waiting for transfers between devices: 0.02 us -> 29.4 us  [body(): lax.all_gather(jnp.concatenate([captions, tag], axis=1), 'mem', axis=0, t...]
    all_to_all x4 -> x3, waiting for transfers between devices: 46.9 us -> 19.3 us  [the longest x1 17.3 us: body(): lax.all_to_all(total, 'grp', split_axis=0, concat_axis=0, tiled=True)]
    unnamed x1 -> x0, blocking collectives: 19.7 us -> none
    all_to_all x4 -> x3, starting transfers between devices: 29.9 us -> 12.2 us  [the longest x1 4.41 us: body(): lax.all_to_all(send_code, 'grp', split_axis=0, concat_axis=0, tiled=True)]
    add x1 -> x2, other arithmetic: 10.7 us -> 0.71 us  [the longest x1 0.7 us: body(): code = clip_bucket * code_base + clip_positive]
    all_to_all x7 -> x3, local copies, waits for them, and re-layouts: 7.95 us -> 1.28 us  [body(): lax.all_to_all(send_code, 'grp', split_axis=0, concat_axis=0, tiled=True)]
    convert_element_type x1 -> x4, other arithmetic: 0.01 us -> 2.92 us  [the longest x1 1.16 us: body(): bucket_y = gathered[:, width].astype(jnp.int32)]
    gather x2 -> x1, local copies, waits for them, and re-layouts: 4.15 us -> 1.27 us  [body(): clip_grad = returned[position].astype(jnp.float32)]
  transfers between devices with their start and end apart: 6 -> 5, of which waited for: 4 -> 4; matrix products, arithmetic and copies ran while one was open for 13% -> 10% of each run, Pallas kernels for 0% -> 0%
where the time goes in v1:
time: 154 us
  waiting for transfers between devices  99.3 us (64%)
  between operations  15.4 us (10%)
  starting transfers between devices  12.3 us (8%)
  matrix products  11.7 us (8%)
  local copies, waits for them, and re-layouts  7.59 us (5%)
  other arithmetic  7.38 us (5%)
    reduce_scatter x1, waiting for transfers between devices, body(): lax.psum_scatter(lax.dot_general(weight, recv_rows, (((0,), (0,)), ((), (...  50.5 us
    all_gather x1, waiting for transfers between devices, body(): lax.all_gather(jnp.concatenate([captions, tag], axis=1), 'mem', axis=0, t...  29.4 us
    all_to_all x1, waiting for transfers between devices, body(): lax.all_to_all(total, 'grp', split_axis=0, concat_axis=0, tiled=True)  17.3 us
    all_to_all x1, starting transfers between devices, body(): lax.all_to_all(send_code, 'grp', split_axis=0, concat_axis=0, tiled=True)  4.41 us
    all_to_all x1, starting transfers between devices, body(): lax.all_to_all(total, 'grp', split_axis=0, concat_axis=0, tiled=True)  4.26 us
    dot_general x1, matrix products, body(): jnp.dot(weight, rows_y, preferred_element_type=jnp.float32)  4.2 us
    dot_general x1, matrix products, inner_rows(): lax.dot_general(left, right, (((1,), (1,)), ((), ())), preferred_element_...  3.86 us
    dot_general x1, matrix products, body(): lax.dot_general(weight, recv_rows, (((0,), (0,)), ((), ())), preferred_el...  3.69 us
  transfers between devices with their start and end apart: 5, of which 4 were waited for; matrix products, arithmetic and copies ran while one was open for 10% of the time, Pallas kernels for 0%

profile of v1, /device:TPU:0, one launch (start us, length us, event | category | flops | bytes accessed | tf_op | source)
XLA Modules:
  0.0 153.7 jit_solution(9011295388158969487)
XLA Ops:
  7.2 0.0 all-gather.2.cloned.1.call-start
  7.2 0.7 convert_element_type.31
  7.9 0.1 broadcast_in_dim.54
  7.9 1.6 %pad_maximum_fusion = bf16[64,1280]{1,0:T(8,128)(2,1)} fusion(bf16[64,128]{1,0:T(8,128)(2,1)S(1)} %broadcast_in_dim.54, bf16[64,1152]{1,0:T(8,128)(2,1)} %param.9), kind=kLoop, calls=%fused_computation.11 | loop fusion | flops 327680 | bytes 327680 | tf_op jit(solution)/shard_map/concatenate | solution.py:45
  9.5 0.0 all-gather.2.cloned.1.call-update
  9.6 0.8 select_reduce_fusion
  10.4 0.6 reduce-window.6
  10.9 0.2 slice_reduce_fusion
  11.2 0.1 fusion.8
  11.3 0.7 multiply_add_fusion
  12.0 1.4 scatter_custom_fusion
  13.4 0.7 all_to_all.24
  14.1 4.4 %all-to-all-start = ((s32[8,64,1]{1,2,0:T(1,128)}), s32[8,64,1]{1,2,0:T(1,128)S(1)}, u32[]{:S(2)}, u32[]{:S(2)}) async-start(s32[8,64,1]{1,2,0:T(1,128)} %bitcast.5), calls=%async_computation | async-start | bytes 8192 | tf_op jit(solution)/shard_map/all_to_all | solution.py:40
  18.5 3.4 %scatter_custom_fusion.1 = bf16[512,1152]{1,0:T(8,128)(2,1)} fusion(s32[256]{0:T(256)S(1)} %bitcast.32, bf16[256,1152]{1,0:T(8,128)(2,1)} %param.8, bf16[]{:T(256)} %constant.57.clone.1), kind=kCustom, calls=%fused_computation.8 | custom fusion | bytes 1180160 | tf_op jit(solution)/shard_map/scatter | solution.py:37
  21.8 1.9 %all-to-all-done = s32[8,64,1]{1,2,0:T(1,128)S(1)} async-done(((s32[8,64,1]{1,2,0:T(1,128)}), s32[8,64,1]{1,2,0:T(1,128)S(1)}, u32[]{:S(2)}, u32[]{:S(2)}) %all-to-all-start) | async-done | bytes 2080 | tf_op jit(solution)/shard_map/all_to_all | solution.py:40
  23.8 3.6 %all-to-all-start.1 = ((bf16[8,64,1152]{2,1,0:T(8,128)(2,1)}), bf16[8,64,1152]{2,1,0:T(8,128)(2,1)S(1)}, u32[]{:S(2)}, u32[]{:S(2)}) async-start(bf16[8,64,1152]{2,1,0:T(8,128)(2,1)} %bitcast.7), calls=%async_computation.1 | async-start | bytes 2359296 | tf_op jit(solution)/shard_map/all_to_all | solution.py:39
  27.4 0.0 reduce-scatter.2.cloned.1.call-start
  28.7 0.5 broadcast.158
  29.3 0.6 reduce.7
  29.9 0.1 all_to_all.26
  30.0 29.4 %all-gather.2.cloned.1.call-done = bf16[1024,1280]{1,0:T(8,128)(2,1)} async-done(((bf16[64,1280]{1,0:T(8,128)(2,1)}), bf16[1024,1280]{1,0:T(8,128)(2,1)}) %all-gather.2.cloned.1.call-update) | async-done | bytes 2621456 | tf_op jit(solution)/shard_map/all_gather | solution.py:45
  59.4 1.2 convert_reduce_fusion
  60.6 0.0 all-to-all-done.1
  60.6 3.9 %select_convert_fusion = bf16[512,1024]{1,0:T(8,128)(2,1)S(1)} fusion(bf16[512,1152]{1,0:T(8,128)(2,1)S(1)} %bitcast.28, bf16[1024,1280]{1,0:T(8,128)(2,1)} %all-gather.2.cloned.1.call-done, f32[]{:T(128)} %bitcast.24, f32[]{:T(128)} %bitcast.23, s32[1024]{0:T(1024)S(1)} %iota_add_fusion, s32[1024]{0:T(1024)S(1)} %convert_reduce_fusion, ...), kind=kOutput, calls=%fused_computation.4 | convolution fusion | flops 1214775296 | bytes 4600832 | tf_op jit(solution)/shard_map/dot_general | solution.py:13
  64.5 3.7 %fusion.15 = f32[1024,1152]{1,0:T(8,128)} fusion(bf16[512,1024]{1,0:T(8,128)(2,1)S(1)} %select_convert_fusion, bf16[512,1152]{1,0:T(8,128)(2,1)S(1)} %bitcast.29), kind=kOutput, calls=%fused_computation.39 | convolution fusion | flops 1207959552 | bytes 6946816 | tf_op jit(solution)/shard_map/dot_general | solution.py:56
  68.2 0.0 reduce-scatter.2.cloned.1.call-update
  68.2 4.2 %convolution_convert_fusion = bf16[512,1152]{1,0:T(8,128)(2,1)} fusion(bf16[512,1024]{1,0:T(8,128)(2,1)S(1)} %select_convert_fusion, bf16[1024,1280]{1,0:T(8,128)(2,1)} %all-gather.2.cloned.1.call-done), kind=kOutput, calls=%fused_computation.3 | convolution fusion | flops 1208549376 | bytes 4587520 | tf_op jit(solution)/shard_map/dot_general | solution.py:54
  72.4 4.3 %all-to-all-start.2 = ((bf16[8,64,1152]{2,1,0:T(8,128)(2,1)}), bf16[8,64,1152]{2,1,0:T(8,128)(2,1)S(1)}, u32[]{:S(2)}, u32[]{:S(2)}) async-start(bf16[8,64,1152]{2,1,0:T(8,128)(2,1)} %bitcast.10), calls=%async_computation.2 | async-start | bytes 2359296 | tf_op jit(solution)/shard_map/all_to_all | solution.py:63
  76.7 17.3 %all-to-all-done.2 = bf16[8,64,1152]{2,1,0:T(8,128)(2,1)S(1)} async-done(((bf16[8,64,1152]{2,1,0:T(8,128)(2,1)}), bf16[8,64,1152]{2,1,0:T(8,128)(2,1)S(1)}, u32[]{:S(2)}, u32[]{:S(2)}) %all-to-all-start.2) | async-done | bytes 1179680 | tf_op jit(solution)/shard_map/all_to_all | solution.py:63
  94.0 1.3 gather_fusion
  95.3 1.1 convert_element_type.36
  96.4 50.5 %reduce-scatter.2.cloned.1.call-done = f32[64,1152]{1,0:T(8,128)} async-done(((f32[1024,1152]{1,0:T(8,128)}), f32[64,1152]{1,0:T(8,128)}) %reduce-scatter.2.cloned.1.call-update) | async-done | bytes 294928 | tf_op jit(solution)/shard_map/reduce_scatter | solution.py:55
  (8 shorter events, 0.1 us)
Async XLA Ops:
  7.2 52.3 %all-gather.2.cloned.1.call-start = ((), (), s32[]{:S(2)}) async-start(), calls=%async_computation.4 | async-start | bytes 2785280 | tf_op jit(solution)/shard_map/all_gather | solution.py:45
  14.1 9.7 %all-to-all-start = ((s32[8,64,1]{1,2,0:T(1,128)}), s32[8,64,1]{1,2,0:T(1,128)S(1)}, u32[]{:S(2)}, u32[]{:S(2)}) async-start(s32[8,64,1]{1,2,0:T(1,128)} %bitcast.5), calls=%async_computation | async-start | bytes 8192 | tf_op jit(solution)/shard_map/all_to_all | solution.py:40
  23.8 36.8 %all-to-all-start.1 = ((bf16[8,64,1152]{2,1,0:T(8,128)(2,1)}), bf16[8,64,1152]{2,1,0:T(8,128)(2,1)S(1)}, u32[]{:S(2)}, u32[]{:S(2)}) async-start(bf16[8,64,1152]{2,1,0:T(8,128)(2,1)} %bitcast.7), calls=%async_computation.1 | async-start | bytes 2359296 | tf_op jit(solution)/shard_map/all_to_all | solution.py:39
  27.4 119.5 %reduce-scatter.2.cloned.1.call-start = ((), (), s32[]{:S(2)}) async-start(), calls=%async_computation.5 | async-start | bytes 5013504 | tf_op jit(solution)/shard_map/reduce_scatter | solution.py:55
  72.4 21.6 %all-to-all-start.2 = ((bf16[8,64,1152]{2,1,0:T(8,128)(2,1)}), bf16[8,64,1152]{2,1,0:T(8,128)(2,1)S(1)}, u32[]{:S(2)}, u32[]{:S(2)}) async-start(bf16[8,64,1152]{2,1,0:T(8,128)(2,1)} %bitcast.10), calls=%async_computation.2 | async-start | bytes 2359296 | tf_op jit(solution)/shard_map/all_to_all | solution.py:63
Sparse Core Ops, SparseCore 0:
  10.7 48.7 all-gather.1
  68.3 78.5 reduce-scatter.1

commit v2 on v1

--- a/solution.py
+++ b/solution.py
@@ -42,7 +42,9 @@
     recv_positive = jnp.where(recv_code >= 0, recv_code % code_base, -1)
     group_index = lax.axis_index("grp")
     tag = jnp.broadcast_to(caption_bucket.astype(captions.dtype)[:, None], (cap_rows, 128))
-    gathered = lax.all_gather(jnp.concatenate([captions, tag], axis=1), "mem", axis=0, tiled=True)
+    own = jnp.concatenate([captions, tag], axis=1)
+    copies = jnp.broadcast_to(own[None], (members,) + own.shape).reshape(members * cap_rows, -1)
+    gathered = lax.all_to_all(copies, "mem", split_axis=0, concat_axis=0, tiled=True)
     rows_y = gathered[:, :width]
     bucket_y = gathered[:, width].astype(jnp.int32)
     count = rows_y.shape[0]
@@ -51,17 +53,14 @@
     weight = pair_weights(
         logits, recv_positive[:, None] == ids[None, :], recv_bucket[:, None] == bucket_y[None, :]
     )
-    total = jnp.dot(weight, rows_y, preferred_element_type=jnp.float32).astype(jnp.bfloat16)
-    caption_grad = lax.psum_scatter(
-        lax.dot_general(
-            weight, recv_rows, (((0,), (0,)), ((), ())), preferred_element_type=jnp.float32
-        ),
-        "mem",
-        scatter_dimension=0,
-        tiled=True,
+    total = jnp.dot(weight, rows_y, preferred_element_type=jnp.float32)
+    partial = lax.dot_general(
+        weight, recv_rows, (((0,), (0,)), ((), ())), preferred_element_type=jnp.float32
     )
+    pieces = lax.all_to_all(partial, "mem", split_axis=0, concat_axis=0, tiled=True)
+    caption_grad = jnp.sum(pieces.reshape(members, cap_rows, width), axis=0)
     returned = lax.all_to_all(total, "grp", split_axis=0, concat_axis=0, tiled=True)
-    clip_grad = returned[position].astype(jnp.float32)
+    clip_grad = returned[position]
     return (clip_grad, caption_grad)
 
 

time: 154 us -> 208 us (1.35)
  waiting for transfers between devices: 99.3 us -> 145 us
  between operations: 15.4 us -> 2.03 us
  starting transfers between devices: 12.3 us -> 24.2 us
  local copies, waits for them, and re-layouts: 7.59 us -> 14.1 us
    all_to_all x0 -> x2, waiting for transfers between devices: none -> 105 us  [the longest x1 68.5 us: body(): lax.all_to_all(partial, 'mem', split_axis=0, concat_axis=0, tiled=True)]
    reduce_scatter x1 -> x0, waiting for transfers between devices: 50.5 us -> none  [body(): lax.psum_scatter(lax.dot_general(weight, recv_rows, (((0,), (0,)), ((), (...]
    all_gather x1 -> x0, waiting for transfers between devices: 29.4 us -> none  [body(): lax.all_gather(jnp.concatenate([captions, tag], axis=1), 'mem', axis=0, t...]
    all_to_all x1, waiting for transfers between devices: 0.01 us -> 13.5 us  [body(): lax.all_to_all(send_rows, 'grp', split_axis=0, concat_axis=0, tiled=True)]
    all_to_all x0 -> x2, starting transfers between devices: none -> 12.6 us  [the longest x1 8.05 us: body(): lax.all_to_all(copies, 'mem', split_axis=0, concat_axis=0, tiled=True)]
    all_to_all x1, waiting for transfers between devices: 17.3 us -> 22.7 us  [body(): lax.all_to_all(total, 'grp', split_axis=0, concat_axis=0, tiled=True)]
    reduce_sum x0 -> x1, other arithmetic: none -> 3.29 us  [body(): caption_grad = jnp.sum(pieces.reshape(members, cap_rows, width), axis=0)]
    convert_element_type x0 -> x1, local copies, waits for them, and re-layouts: none -> 2.28 us  [pair_weights(): jnp.where(same, -sign * jax.nn.sigmoid(-sign * logits), 0.0)]
  transfers between devices with their start and end apart: 5 -> 5, of which waited for: 4 -> 5; matrix products, arithmetic and copies ran while one was open for 10% -> 8% of each run, Pallas kernels for 0% -> 0%
where the time goes in v2:
time: 208 us
  waiting for transfers between devices  145 us (70%)
  starting transfers between devices  24.2 us (12%)
  local copies, waits for them, and re-layouts  14.1 us (7%)
  matrix products  13.6 us (7%)
  other arithmetic  8.9 us (4%)
    all_to_all x1, waiting for transfers between devices, body(): lax.all_to_all(partial, 'mem', split_axis=0, concat_axis=0, tiled=True)  68.5 us
    all_to_all x1, waiting for transfers between devices, body(): lax.all_to_all(copies, 'mem', split_axis=0, concat_axis=0, tiled=True)  36.5 us
    all_to_all x1, waiting for transfers between devices, body(): lax.all_to_all(total, 'grp', split_axis=0, concat_axis=0, tiled=True)  22.7 us
    all_to_all x1, waiting for transfers between devices, body(): lax.all_to_all(send_rows, 'grp', split_axis=0, concat_axis=0, tiled=True)  13.5 us
    all_to_all x1, starting transfers between devices, body(): lax.all_to_all(copies, 'mem', split_axis=0, concat_axis=0, tiled=True)  8.05 us
    dot_general x1, matrix products, inner_rows(): lax.dot_general(left, right, (((1,), (1,)), ((), ())), preferred_element_...  4.97 us
    dot_general x1, matrix products, body(): lax.dot_general(weight, recv_rows, (((0,), (0,)), ((), ())), preferred_el...  4.87 us
    all_to_all x1, starting transfers between devices, body(): lax.all_to_all(partial, 'mem', split_axis=0, concat_axis=0, tiled=True)  4.56 us
  transfers between devices with their start and end apart: 5, of which 5 were waited for; matrix products, arithmetic and copies ran while one was open for 8% of the time, Pallas kernels for 0%

profile of v2, /device:TPU:0, one launch (start us, length us, event | category | flops | bytes accessed | tf_op | source)
XLA Modules:
  0.0 207.6 jit_solution(651500156255665370)
XLA Ops:
  0.6 0.8 select_reduce_fusion
  1.4 0.7 multiply_add_fusion.1
  2.1 0.6 reduce-window.6
  2.7 0.2 slice_reduce_fusion
  2.9 0.1 fusion.23
  3.1 1.4 scatter_custom_fusion
  4.5 0.7 all_to_all.34
  5.1 4.4 %all-to-all-start = ((s32[8,64,1]{1,2,0:T(1,128)}), s32[8,64,1]{1,2,0:T(1,128)S(1)}, u32[]{:S(2)}, u32[]{:S(2)}) async-start(s32[8,64,1]{1,2,0:T(1,128)} %bitcast.5), calls=%async_computation | async-start | bytes 8192 | tf_op jit(solution)/shard_map/all_to_all | solution.py:40
  9.5 0.7 convert_element_type.28
  10.2 0.1 broadcast_in_dim.66
  10.3 0.9 pad_maximum_fusion
  11.2 3.6 %all-to-all-done = s32[8,64,1]{1,2,0:T(1,128)S(1)} async-done(((s32[8,64,1]{1,2,0:T(1,128)}), s32[8,64,1]{1,2,0:T(1,128)S(1)}, u32[]{:S(2)}, u32[]{:S(2)}) %all-to-all-start) | async-done | bytes 2080 | tf_op jit(solution)/shard_map/all_to_all | solution.py:40
  14.8 1.8 broadcast_in_dim.67
  16.5 8.0 %all-to-all-start.1 = ((bf16[16,64,1280]{2,1,0:T(8,128)(2,1)}), bf16[16,64,1280]{2,1,0:T(8,128)(2,1)S(1)}, u32[]{:S(2)}, u32[]{:S(2)}) async-start(bf16[16,64,1280]{2,1,0:T(8,128)(2,1)} %broadcast_in_dim.67), calls=%async_computation.1 | async-start | bytes 5242880 | tf_op jit(solution)/shard_map/all_to_all | solution.py:47
  24.6 3.4 %scatter_custom_fusion.1 = bf16[512,1152]{1,0:T(8,128)(2,1)} fusion(s32[256]{0:T(256)S(1)} %bitcast.58, bf16[256,1152]{1,0:T(8,128)(2,1)} %param.8, bf16[]{:T(256)} %constant.57.clone.1), kind=kCustom, calls=%fused_computation.26 | custom fusion | bytes 1180160 | tf_op jit(solution)/shard_map/scatter | solution.py:37
  27.9 36.5 %all-to-all-done.1 = bf16[16,64,1280]{2,1,0:T(8,128)(2,1)S(1)} async-done(((bf16[16,64,1280]{2,1,0:T(8,128)(2,1)}), bf16[16,64,1280]{2,1,0:T(8,128)(2,1)S(1)}, u32[]{:S(2)}, u32[]{:S(2)}) %all-to-all-start.1) | async-done | bytes 2621472 | tf_op jit(solution)/shard_map/all_to_all | solution.py:47
  64.4 0.0 copy-start
  64.4 1.5 copy-done
  65.9 3.6 %all-to-all-start.2 = ((bf16[8,64,1152]{2,1,0:T(8,128)(2,1)}), bf16[8,64,1152]{2,1,0:T(8,128)(2,1)S(1)}, u32[]{:S(2)}, u32[]{:S(2)}) async-start(bf16[8,64,1152]{2,1,0:T(8,128)(2,1)} %bitcast.8), calls=%async_computation.2 | async-start | bytes 2359296 | tf_op jit(solution)/shard_map/all_to_all | solution.py:39
  70.8 0.6 broadcast.172
  71.4 0.6 reduce.8
  72.0 0.1 all_to_all.36
  72.1 1.2 convert_reduce_fusion
  73.3 13.5 %all-to-all-done.2 = bf16[8,64,1152]{2,1,0:T(8,128)(2,1)S(1)} async-done(((bf16[8,64,1152]{2,1,0:T(8,128)(2,1)}), bf16[8,64,1152]{2,1,0:T(8,128)(2,1)S(1)}, u32[]{:S(2)}, u32[]{:S(2)}) %all-to-all-start.2) | async-done | bytes 1179680 | tf_op jit(solution)/shard_map/all_to_all | solution.py:39
  86.8 0.0 copy-start.1
  86.8 5.0 %fusion.6 = (bf16[1024,512]{0,1:T(8,128)(2,1)}, f32[512,1024]{1,0:T(8,128)S(1)}) fusion(s32[1024]{0:T(1024)S(1)} %iota_add_fusion, s32[1024]{0:T(1024)S(1)} %convert_reduce_fusion, f32[]{:T(128)} %bitcast.45, f32[]{:T(128)} %bitcast.43, s32[512]{0:T(512)S(1)} %get-tuple-element.3, s32[512]{0:T(512)S(1)} %get-tuple-element.2, ...), kind=kOutput, calls=%fused_computation.12 | convolution fusion | flops 1214775296 | bytes 6697984 | tf_op jit(solution)/shard_map/dot_general | solution.py:13
  91.7 0.0 copy-done.1
  91.7 3.8 %fusion.7 = f32[512,1152]{1,0:T(8,128)} fusion(bf16[1024,1280]{1,0:T(8,128)(2,1)S(1)} %bitcast.54, f32[512,1024]{1,0:T(8,128)S(1)} %get-tuple-element.5, f32[]{:T(128)} %bitcast.44, f32[]{:T(128)} %bitcast.42, s32[1024]{0:T(1024)S(1)} %iota_add_fusion, s32[1024]{0:T(1024)S(1)} %convert_reduce_fusion, s32[512]{0:T(512)S(1)} %get-tuple-element.3, ...), kind=kOutput, calls=%fused_computation.13 | convolution fusion | flops 1214775296 | bytes 6828040 | tf_op jit(solution)/shard_map/dot_general | solution.py:56
  95.5 3.6 %all-to-all-start.3 = ((f32[8,64,1152]{2,1,0:T(8,128)}), f32[8,64,1152]{2,1,0:T(8,128)S(1)}, u32[]{:S(2)}, u32[]{:S(2)}) async-start(f32[8,64,1152]{2,1,0:T(8,128)} %bitcast.55), calls=%async_computation.3 | async-start | bytes 4718592 | tf_op jit(solution)/shard_map/all_to_all | solution.py:62
  99.1 2.3 %copy.17 = bf16[1024,512]{1,0:T(8,128)(2,1)} copy(bf16[1024,512]{0,1:T(8,128)(2,1)} %get-tuple-element.4) | data formatting | bytes 2097152 | tf_op jit(solution)/shard_map/convert_element_type | solution.py:9
  101.4 4.9 %fusion.33 = f32[16,64,1152]{2,1,0:T(8,128)} fusion(bf16[16,64,512]{2,1,0:T(8,128)(2,1)} %bitcast.51, bf16[512,1152,1]{1,0,2:T(8,128)(2,1)S(1)} %bitcast.50), kind=kOutput, calls=%fused_computation.60 | convolution fusion | flops 1207959552 | bytes 6946816 | tf_op jit(solution)/shard_map/dot_general | solution.py:57
  106.3 22.7 %all-to-all-done.3 = f32[8,64,1152]{2,1,0:T(8,128)S(1)} async-done(((f32[8,64,1152]{2,1,0:T(8,128)}), f32[8,64,1152]{2,1,0:T(8,128)S(1)}, u32[]{:S(2)}, u32[]{:S(2)}) %all-to-all-start.3) | async-done | bytes 2359328 | tf_op jit(solution)/shard_map/all_to_all | solution.py:62
  129.0 4.6 %all-to-all-start.4 = ((f32[16,64,1152]{2,1,0:T(8,128)}), f32[16,64,1152]{2,1,0:T(8,128)}, u32[]{:S(2)}, u32[]{:S(2)}) async-start(f32[16,64,1152]{2,1,0:T(8,128)} %fusion.33), calls=%async_computation.4 | async-start | bytes 9437184 | tf_op jit(solution)/shard_map/all_to_all | solution.py:60
  133.6 2.2 %gather_fusion = f32[256,1152]{1,0:T(8,128)} fusion(f32[512,1152]{1,0:T(8,128)S(1)} %bitcast.48, s32[1024]{0:T(1024)S(1)} %pad_clamp_fusion), kind=kCustom, calls=%fused_computation | custom fusion | bytes 2360320 | tf_op jit(solution)/shard_map/gather | solution.py:63
  135.8 68.5 %all-to-all-done.4 = f32[16,64,1152]{2,1,0:T(8,128)} async-done(((f32[16,64,1152]{2,1,0:T(8,128)}), f32[16,64,1152]{2,1,0:T(8,128)}, u32[]{:S(2)}, u32[]{:S(2)}) %all-to-all-start.4) | async-done | bytes 4718624 | tf_op jit(solution)/shard_map/all_to_all | solution.py:60
  204.3 3.3 %reduce_sum.29 = f32[64,1152]{1,0:T(8,128)} reduce(f32[16,64,1152]{2,1,0:T(8,128)} %all-to-all-done.4, f32[]{:T(128)} %constant.58.clone.1), dimensions={0}, to_apply=%region_6.7 | reduce | flops 1105920 | bytes 5013508 | tf_op jit(solution)/shard_map/reduce_sum | solution.py:61
  (8 shorter events, 0.1 us)
Async XLA Ops:
  5.1 9.6 %all-to-all-start = ((s32[8,64,1]{1,2,0:T(1,128)}), s32[8,64,1]{1,2,0:T(1,128)S(1)}, u32[]{:S(2)}, u32[]{:S(2)}) async-start(s32[8,64,1]{1,2,0:T(1,128)} %bitcast.5), calls=%async_computation | async-start | bytes 8192 | tf_op jit(solution)/shard_map/all_to_all | solution.py:40
  16.5 47.9 %all-to-all-start.1 = ((bf16[16,64,1280]{2,1,0:T(8,128)(2,1)}), bf16[16,64,1280]{2,1,0:T(8,128)(2,1)S(1)}, u32[]{:S(2)}, u32[]{:S(2)}) async-start(bf16[16,64,1280]{2,1,0:T(8,128)(2,1)} %broadcast_in_dim.67), calls=%async_computation.1 | async-start | bytes 5242880 | tf_op jit(solution)/shard_map/all_to_all | solution.py:47
  64.4 1.5 copy-start
  65.9 20.8 %all-to-all-start.2 = ((bf16[8,64,1152]{2,1,0:T(8,128)(2,1)}), bf16[8,64,1152]{2,1,0:T(8,128)(2,1)S(1)}, u32[]{:S(2)}, u32[]{:S(2)}) async-start(bf16[8,64,1152]{2,1,0:T(8,128)(2,1)} %bitcast.8), calls=%async_computation.2 | async-start | bytes 2359296 | tf_op jit(solution)/shard_map/all_to_all | solution.py:39
  86.8 5.0 %copy-start.1 = (bf16[16,64,1280]{2,1,0:T(8,128)(2,1)S(1)}, bf16[16,64,1280]{2,1,0:T(8,128)(2,1)}, u32[]{:S(2)}) copy-start(bf16[16,64,1280]{2,1,0:T(8,128)(2,1)} %copy-done) | copy-start | bytes 7864324
  95.5 33.5 %all-to-all-start.3 = ((f32[8,64,1152]{2,1,0:T(8,128)}), f32[8,64,1152]{2,1,0:T(8,128)S(1)}, u32[]{:S(2)}, u32[]{:S(2)}) async-start(f32[8,64,1152]{2,1,0:T(8,128)} %bitcast.55), calls=%async_computation.3 | async-start | bytes 4718592 | tf_op jit(solution)/shard_map/all_to_all | solution.py:62
  129.0 75.3 %all-to-all-start.4 = ((f32[16,64,1152]{2,1,0:T(8,128)}), f32[16,64,1152]{2,1,0:T(8,128)}, u32[]{:S(2)}, u32[]{:S(2)}) async-start(f32[16,64,1152]{2,1,0:T(8,128)} %fusion.33), calls=%async_computation.4 | async-start | bytes 9437184 | tf_op jit(solution)/shard_map/all_to_all | solution.py:60
